TPU v7x, 256 devices: a whole 4x4x8 slice. The times are simulated.
256 devices in a mesh: blk: 32 (over x, y, core), req: 8 (over z).
Axes of the slice: x: 4, y: 4, z: 8, core: 2. Of those that a mesh axis runs over, the one named last changes fastest.
Arguments:
- patches: bfloat16 [6144, 1408], P('req')
- vis_ln_gain: bfloat16 [1408], replicated, may hold values from 0.25 to 4
- vis_ln_bias: bfloat16 [1408], replicated, may hold values from -3 to 3
- vis_up: bfloat16 [1408, 6144], P(None, 'blk'), may hold values from -0.15625 to 0.15625
- vis_up_bias: bfloat16 [6144], P('blk'), may hold values from -3 to 3
- vis_down: bfloat16 [6144, 1408], P('blk'), may hold values from -0.15625 to 0.15625
- vis_down_bias: bfloat16 [1408], replicated, may hold values from -3 to 3
- merge_gain: bfloat16 [1408], replicated, may hold values from 0.099609375 to 1.8984375
- merge_proj: bfloat16 [5632, 4096], P(None, 'blk'), may hold values from -0.078125 to 0.078125
- merge_proj_bias: bfloat16 [4096], P('blk'), may hold values from -3 to 3
- image_dest: int32 [1536], replicated, may hold values from 0 to 8191, as said below
- text_embed: bfloat16 [8192, 4096], P('req', 'blk')
- segment_ids: int32 [8, 1024], P('req'), may hold values from 0 to 3, never falling along the last dimension, each value on 1 to 512 neighbouring positions
- text_gain: bfloat16 [4096], replicated, may hold values from 0.099609375 to 1.8984375
- query_weight: bfloat16 [4096, 4096], P(None, 'blk')
- key_weight: bfloat16 [4096, 4096], P(None, 'blk')
- value_weight: bfloat16 [4096, 4096], P(None, 'blk'), may hold values from -0.09375 to 0.09375
- out_weight: bfloat16 [4096, 4096], P('blk'), may hold values from -0.1875 to 0.1875
Outputs:
- hidden_out: bfloat16 [8192, 4096], P(('req', 'blk'))
Inputs may be any that keep to these rules, and one draw needn't show every extreme that they name: image_dest holds distinct positions; each group of 1024 positions receives exactly 192 image rows, and of one group's 192 image rows at most 66 go to one group of positions, exactly 66 for one group. `segment_ids`: each row has 4 requests as runs of equal, non-decreasing ids, each of 1 to 512 tokens, one exactly 512.
All inputs are finite; a program needn't handle non-finite values.
Results may differ from a plain program's by a relative error of at most 0.04.
Values may be sent and summed in bfloat16 or wider, within the bound.
No kernel may reach another device: no remote copies, remote signals or barrier semaphores. Data moves between devices by JAX's collectives and lax.ppermute only.
A program may use at most 128 MiB of HBM per device.

v0:
```python
import jax
import jax.numpy as jnp
from jax import lax
from jax.sharding import PartitionSpec as P

HEAD = 128


def layer_norm(values, gain_vector, shift_vector):
    centre = jnp.mean(values, axis=-1, keepdims=True)
    centred = values - centre
    spread = jnp.mean(centred * centred, axis=-1, keepdims=True)
    result = centred * lax.rsqrt(spread + 1e-06) * gain_vector.astype(jnp.float32)
    if shift_vector is None:
        return result
    return result + shift_vector.astype(jnp.float32)


def rotate(values, positions):
    half_size = HEAD // 2
    frequency = 10000.0 ** (-2.0 * jnp.arange(half_size, dtype=jnp.float32) / HEAD)
    angles = positions.astype(jnp.float32)[:, None] * frequency[None, :]
    cosine = jnp.cos(angles)[:, None, :]
    sine_table = jnp.sin(angles)[:, None, :]
    by_head = values.reshape(values.shape[0], -1, HEAD)
    first_half = by_head[..., :half_size]
    second_half = by_head[..., half_size:]
    turned = jnp.concatenate(
        [
            first_half * cosine - second_half * sine_table,
            second_half * cosine + first_half * sine_table,
        ],
        axis=-1,
    )
    return turned.reshape(values.shape)


def causal_setup(segments):
    length = segments.shape[0]
    column_ids = jnp.arange(length)
    same_request = segments[:, None] == segments[None, :]
    earlier = column_ids[None, :] < column_ids[:, None]
    positions = jnp.sum(same_request & earlier, axis=1)
    allowed = same_request & (column_ids[None, :] <= column_ids[:, None])
    return (positions, allowed)


def attend(queries, keys, values, allowed):
    row_count = queries.shape[0]
    key_count = keys.shape[0]
    query_heads = queries.reshape(row_count, -1, HEAD)
    key_heads = keys.reshape(key_count, -1, HEAD)
    value_heads = values.reshape(key_count, -1, HEAD)
    scores = jnp.einsum(
        "thd,shd->hts", query_heads, key_heads, preferred_element_type=jnp.float32
    ) * HEAD ** (-0.5)
    scores = jnp.where(allowed[None, :, :], scores, -jnp.inf)
    top_score = jnp.max(scores, axis=-1, keepdims=True)
    weights = jnp.exp(scores - top_score)
    weights = (weights / jnp.sum(weights, axis=-1, keepdims=True)).astype(jnp.bfloat16)
    mixed = jnp.einsum("hts,shd->thd", weights, value_heads, preferred_element_type=jnp.float32)
    return mixed.astype(jnp.bfloat16).reshape(row_count, -1)


def body(
    patches,
    vis_ln_gain,
    vis_ln_bias,
    vis_up,
    vis_up_bias,
    vis_down,
    vis_down_bias,
    merge_gain,
    merge_proj,
    merge_proj_bias,
    image_dest,
    text_embed,
    segment_ids,
    text_gain,
    query_weight,
    key_weight,
    value_weight,
    out_weight,
):
    blk_count = lax.axis_size("blk")
    req_count = lax.axis_size("req")
    blk_index = lax.axis_index("blk")
    req_index = lax.axis_index("req")
    vis_width = patches.shape[1]
    patch_rows = patches.astype(jnp.float32)
    normed = layer_norm(patch_rows, vis_ln_gain, vis_ln_bias).astype(jnp.bfloat16)
    pre_act = jnp.dot(normed, vis_up, preferred_element_type=jnp.float32) + vis_up_bias.astype(
        jnp.float32
    )
    hidden = jax.nn.gelu(pre_act, approximate=False).astype(jnp.bfloat16)
    summed = lax.psum(
        jnp.dot(hidden, vis_down, preferred_element_type=jnp.float32).astype(jnp.bfloat16), "blk"
    ).astype(jnp.float32)
    vis_out = patches.astype(jnp.float32) + summed + vis_down_bias.astype(jnp.float32)
    normed = layer_norm(vis_out, merge_gain, None).astype(jnp.bfloat16)
    image_cols = jnp.dot(
        normed.reshape(-1, 4 * vis_width), merge_proj, preferred_element_type=jnp.float32
    )
    image_cols = (image_cols + merge_proj_bias.astype(jnp.float32)).astype(jnp.bfloat16)
    image_count = image_cols.shape[0]
    col_width = image_cols.shape[1]
    tok_grp = text_embed.shape[0]
    dest_group = image_dest // tok_grp
    dest_local = image_dest - dest_group * tok_grp
    target = jnp.where(dest_group == req_index, dest_local, tok_grp)
    filler = jnp.zeros((1, col_width), jnp.bfloat16)
    capacity = image_count // 4 + 3 * image_count // 4 // req_count
    by_source = dest_group.reshape(req_count, image_count)
    one_hot = (
        by_source[:, :, None] == jnp.arange(req_count, dtype=jnp.int32)[None, None, :]
    ).astype(jnp.int32)
    slot_index = jnp.sum((jnp.cumsum(one_hot, axis=1) - one_hot) * one_hot, axis=2)
    send_slot = lax.dynamic_index_in_dim(
        by_source * capacity + slot_index, req_index, 0, keepdims=False
    )
    source_row = (
        jnp.full((req_count * capacity,), image_count, jnp.int32)
        .at[send_slot]
        .set(jnp.arange(image_count, dtype=jnp.int32))
    )
    outgoing = jnp.take(jnp.concatenate([image_cols, filler], axis=0), source_row, axis=0)
    incoming = lax.all_to_all(outgoing, "req", split_axis=0, concat_axis=0, tiled=True)
    arrival = (jnp.arange(req_count, dtype=jnp.int32)[:, None] * capacity + slot_index).reshape(-1)
    row_table = jnp.concatenate([incoming, filler], axis=0)
    missing = row_table.shape[0] - 1
    lookup = jnp.full((tok_grp,), missing, jnp.int32).at[target].set(arrival, mode="drop")
    columns = jnp.where(
        (lookup < missing)[:, None], jnp.take(row_table, lookup, axis=0), text_embed
    )
    features = lax.all_gather(columns, "blk", axis=1, tiled=True)
    token_values = features.astype(jnp.float32)
    normed_tokens = (
        token_values
        * lax.rsqrt(jnp.mean(token_values * token_values, axis=-1, keepdims=True) + 1e-05)
        * text_gain.astype(jnp.float32)
    ).astype(jnp.bfloat16)
    positions, allowed = causal_setup(segment_ids[0])
    queries = rotate(
        jnp.dot(normed_tokens, query_weight, preferred_element_type=jnp.float32), positions
    ).astype(jnp.bfloat16)
    keys_rot = rotate(
        jnp.dot(normed_tokens, key_weight, preferred_element_type=jnp.float32), positions
    ).astype(jnp.bfloat16)
    values_here = jnp.dot(normed_tokens, value_weight, preferred_element_type=jnp.float32).astype(
        jnp.bfloat16
    )
    block_rows = min(512, tok_grp)
    block_count = tok_grp // block_rows

    def attend_block(block_pair):
        return attend(block_pair[0], keys_rot, values_here, block_pair[1])

    attn_out = lax.map(
        attend_block,
        (
            queries.reshape(block_count, block_rows, -1),
            allowed.reshape(block_count, block_rows, tok_grp),
        ),
    ).reshape(tok_grp, -1)
    out_share = tok_grp // blk_count
    summed_heads = lax.psum_scatter(
        jnp.dot(attn_out, out_weight, preferred_element_type=jnp.float32).astype(jnp.bfloat16),
        "blk",
        scatter_dimension=0,
        tiled=True,
    ).astype(jnp.float32)
    residual = lax.dynamic_slice_in_dim(token_values, blk_index * out_share, out_share, 0)
    return (residual + summed_heads).astype(jnp.bfloat16)


def solution(mesh):
    return jax.shard_map(
        body,
        mesh=mesh,
        in_specs=(
            P("req", None),
            P(),
            P(),
            P(None, "blk"),
            P("blk"),
            P("blk", None),
            P(),
            P(),
            P(None, "blk"),
            P("blk"),
            P(),
            P("req", "blk"),
            P("req", None),
            P(),
            P(None, "blk"),
            P(None, "blk"),
            P(None, "blk"),
            P("blk", None),
        ),
        out_specs=P(("req", "blk"), None),
        check_vma=False,
    )
```

profile of v0, /device:TPU:2, one launch (start us, length us, event | category | flops | bytes accessed | tf_op | source)
XLA Modules:
  0.0 381.4 jit_solution(12648237813361242620)
XLA Ops:
  7.4 2.0 convert_reduce_fusion
  9.4 2.3 fusion.9
  11.8 6.3 %convolution_convert_fusion.2 = bf16[768,1408]{1,0:T(8,128)(2,1)} fusion(bf16[192,1408]{1,0:T(8,128)(2,1)S(1)} %copy-done.17, bf16[1408,192]{0,1:T(8,128)(2,1)S(1)} %copy-done.18, bf16[768,1408]{1,0:T(8,128)(2,1)} %param.20, f32[1408]{0:T(1024)S(1)} %convert_element_type.103, f32[1408]{0:T(1024)S(1)} %convert_element_type.102, ...), kind=kOutput, calls=%fused_computation.35 | convolution fusion | flops 847773696 | bytes 5424896 | tf_op jit(solution)/shard_map/dot_general | solution.py:97
  18.4 4.5 %reduce-window.6 = s32[8,8,2,128]{3,1,2,0:T(8,128)S(1)} reduce-window(s32[8,8,2,128]{3,1,2,0:T(8,128)S(1)} %convert_bitcast_fusion, s32[]{:T(128)} %constant.42.clone.1), window={size=1x1x1x128 pad=0_0x0_0x0_0x127_0}, to_apply=%region_0.0 | reduce-window | flops 2080768 | bytes 131076 | tf_op jit(solution)/shard_map/reduce-window
  24.8 6.2 %scatter_custom_fusion = s32[1024]{0:T(1024)S(1)} fusion(s32[1536]{0:T(1024)S(1)} %get-tuple-element.74, s32[1536]{0:T(1024)S(1)} %reshape.297, s32[]{:T(128)} %constant.68.clone.1), kind=kCustom, calls=%fused_computation.151 | custom fusion | bytes 4100 | tf_op jit(solution)/shard_map/scatter | solution.py:131
  31.0 107.0 %all-reduce.5.cloned.1.call-done = bf16[768,1408]{1,0:T(8,128)(2,1)} async-done(((bf16[768,1408]{1,0:T(8,128)(2,1)}), bf16[768,1408]{1,0:T(8,128)(2,1)}) %all-reduce.5.cloned.1.call-update) | async-done | bytes 2162704 | tf_op jit(solution)/shard_map/psum | solution.py:96
  138.0 3.2 fusion.16
  142.7 2.4 multiply_convert_fusion.1
  145.1 4.4 %reshape.272 = bf16[192,5632]{1,0:T(8,128)(2,1)} reshape(bf16[768,1408]{1,0:T(8,128)(2,1)} %multiply_convert_fusion.1) | data formatting | bytes 4325376 | tf_op jit(solution)/shard_map/reshape | solution.py:102
  149.6 2.4 fusion.22
  151.9 1.9 gather_fusion
  154.7 7.0 %all-to-all-start = ((bf16[8,66,128]{2,1,0:T(8,128)(2,1)}), bf16[8,66,128]{2,1,0:T(8,128)(2,1)S(1)}, u32[]{:S(2)}, u32[]{:S(2)}) async-start(bf16[8,66,128]{2,1,0:T(8,128)(2,1)} %broadcast_select_fusion), calls=%async_computation | async-start | bytes 294912 | tf_op jit(solution)/shard_map/all_to_all | solution.py:127
  161.8 9.6 %all-to-all-done = bf16[8,66,128]{2,1,0:T(8,128)(2,1)S(1)} async-done(((bf16[8,66,128]{2,1,0:T(8,128)(2,1)}), bf16[8,66,128]{2,1,0:T(8,128)(2,1)S(1)}, u32[]{:S(2)}, u32[]{:S(2)}) %all-to-all-start) | async-done | bytes 135200 | tf_op jit(solution)/shard_map/all_to_all | solution.py:127
  171.5 3.2 gather_fusion.1
  179.0 55.5 %all-gather.2.cloned.1.call-done = bf16[1024,4096]{1,0:T(8,128)(2,1)} async-done(((bf16[1024,128]{1,0:T(8,128)(2,1)}), bf16[1024,4096]{1,0:T(8,128)(2,1)}) %all-gather.2.cloned.1.call-update) | async-done | bytes 8388624 | tf_op jit(solution)/shard_map/all_gather | solution.py:135
  234.5 5.1 %multiply_reduce_fusion = f32[1024]{0:T(1024)S(1)} fusion(bf16[1024,4096]{1,0:T(8,128)(2,1)} %all-gather.2.cloned.1.call-done), kind=kLoop, calls=%fused_computation.16 | loop fusion | flops 12581888 | bytes 8392704 | tf_op jit(solution)/shard_map/reduce_sum | solution.py:139
  239.6 10.4 %multiply_convert_fusion = bf16[1024,4096]{1,0:T(8,128)(2,1)} fusion(f32[4096]{0:T(1024)S(1)} %convert_element_type.115, f32[1024]{0:T(1024)S(1)} %add_rsqrt_fusion, bf16[1024,4096]{1,0:T(8,128)(2,1)} %all-gather.2.cloned.1.call-done), kind=kLoop, calls=%fused_computation.15 | loop fusion | flops 16777216 | bytes 16797696 | tf_op jit(solution)/shard_map/convert_element_type | solution.py:141
  250.1 5.9 %convolution_convert_fusion.3 = bf16[1024,128]{1,0:T(8,128)(2,1)S(1)} fusion(bf16[1024,4096]{1,0:T(8,128)(2,1)} %multiply_convert_fusion, bf16[4096,128]{1,0:T(8,128)(2,1)S(1)} %copy-done.16), kind=kOutput, calls=%fused_computation.41 | convolution fusion | flops 1073872896 | bytes 9699328 | tf_op jit(solution)/shard_map/dot_general | solution.py:149
  256.1 2.9 convolution_bitcast_fusion
  259.0 2.9 convolution_bitcast_fusion.1
  263.7 3.4 while.10
  267.2 5.5 %convolution_convert_fusion.1 = bf16[1024,4096]{1,0:T(8,128)(2,1)} fusion(bf16[1024,128]{1,0:T(8,128)(2,1)S(1)} %bitcast.70, bf16[128,4096]{1,0:T(8,128)(2,1)S(1)} %copy-done.7), kind=kOutput, calls=%fused_computation.17 | convolution fusion | flops 1077936128 | bytes 9699328 | tf_op jit(solution)/shard_map/dot_general | solution.py:167
  272.8 11.5 %convert_element_type.114 = f32[1024,4096]{1,0:T(8,128)} convert(bf16[1024,4096]{1,0:T(8,128)(2,1)} %all-gather.2.cloned.1.call-done) | non-fusion elementwise | flops 4194304 | bytes 25165824 | tf_op jit(solution)/shard_map/convert_element_type | solution.py:136
  284.3 88.8 %reduce-scatter.2.cloned.1.call-done = bf16[32,4096]{1,0:T(8,128)(2,1)} async-done(((bf16[1024,4096]{1,0:T(8,128)(2,1)}), bf16[32,4096]{1,0:T(8,128)(2,1)}) %reduce-scatter.2.cloned.1.call-update) | async-done | bytes 262160 | tf_op jit(solution)/shard_map/reduce_scatter | solution.py:166
  (109 shorter events, 16.8 us)
Async XLA Ops:
  6.5 143.0 %copy-start = (bf16[5632,128]{1,0:T(8,128)(2,1)S(1)}, bf16[5632,128]{1,0:T(8,128)(2,1)}, u32[]{:S(2)}) copy-start(bf16[5632,128]{1,0:T(8,128)(2,1)} %param.28) | copy-start | bytes 4325380
  6.5 5.2 %copy-start.12 = (bf16[1408]{0:T(1024)(128)(2,1)S(1)}, bf16[1408]{0:T(1024)(128)(2,1)}, u32[]{:S(2)}) copy-start(bf16[1408]{0:T(1024)(128)(2,1)} %param.21) | copy-start | bytes 8452
  6.5 5.2 %copy-start.13 = (bf16[1408]{0:T(1024)(128)(2,1)S(1)}, bf16[1408]{0:T(1024)(128)(2,1)}, u32[]{:S(2)}) copy-start(bf16[1408]{0:T(1024)(128)(2,1)} %param.22) | copy-start | bytes 8452
  6.5 5.2 %copy-start.17 = (bf16[192,1408]{1,0:T(8,128)(2,1)S(1)}, bf16[192,1408]{1,0:T(8,128)(2,1)}, u32[]{:S(2)}) copy-start(bf16[192,1408]{1,0:T(8,128)(2,1)} %param.25) | copy-start | bytes 1622020
  6.5 5.2 %copy-start.18 = (bf16[1408,192]{0,1:T(8,128)(2,1)S(1)}, bf16[1408,192]{0,1:T(8,128)(2,1)}, u32[]{:S(2)}) copy-start(bf16[1408,192]{0,1:T(8,128)(2,1)} %param.23) | copy-start | bytes 1622020
  6.5 131.5 %all-reduce.5.cloned.1.call-start = ((), (), s32[]{:S(2)}) async-start(), calls=%async_computation.2 | async-start | bytes 4325376 | tf_op jit(solution)/shard_map/psum | solution.py:96
  11.8 6.4 %copy-start.19 = (bf16[128]{0:T(256)(128)(2,1)S(1)}, bf16[128]{0:T(256)(128)(2,1)}, u32[]{:S(2)}) copy-start(bf16[128]{0:T(256)(128)(2,1)} %param.29) | copy-start | bytes 772
  11.8 6.4 %copy-start.14 = (bf16[1408]{0:T(1024)(128)(2,1)S(1)}, bf16[1408]{0:T(1024)(128)(2,1)}, u32[]{:S(2)}) copy-start(bf16[1408]{0:T(1024)(128)(2,1)} %param.26) | copy-start | bytes 8452
  11.8 6.4 %copy-start.15 = (bf16[1408]{0:T(1024)(128)(2,1)S(1)}, bf16[1408]{0:T(1024)(128)(2,1)}, u32[]{:S(2)}) copy-start(bf16[1408]{0:T(1024)(128)(2,1)} %param.27) | copy-start | bytes 8452
  11.8 6.4 %copy-start.10 = (s32[1536]{0:T(1024)S(1)}, s32[1536]{0:T(1024)}, u32[]{:S(2)}) copy-start(s32[1536]{0:T(1024)} %param.30) | copy-start | bytes 18436
  138.0 3.2 copy-start.3
  138.0 3.6 copy-start.4
  149.5 25.2 %copy-start.8 = (bf16[1024,128]{1,0:T(8,128)(2,1)S(1)}, bf16[1024,128]{1,0:T(8,128)(2,1)}, u32[]{:S(2)}) copy-start(bf16[1024,128]{1,0:T(8,128)(2,1)} %param.31) | copy-start | bytes 786436
  149.6 26.8 %copy-start.9 = (s32[1,1024]{1,0:T(1,128)S(1)}, s32[1,1024]{1,0:T(1,128)}, u32[]{:S(2)}) copy-start(s32[1,1024]{1,0:T(1,128)} %param.32) | copy-start | bytes 12292
  149.6 28.0 %copy-start.11 = (bf16[4096]{0:T(1024)(128)(2,1)S(1)}, bf16[4096]{0:T(1024)(128)(2,1)}, u32[]{:S(2)}) copy-start(bf16[4096]{0:T(1024)(128)(2,1)} %param.33) | copy-start | bytes 24580
  154.7 16.7 %all-to-all-start = ((bf16[8,66,128]{2,1,0:T(8,128)(2,1)}), bf16[8,66,128]{2,1,0:T(8,128)(2,1)S(1)}, u32[]{:S(2)}, u32[]{:S(2)}) async-start(bf16[8,66,128]{2,1,0:T(8,128)(2,1)} %broadcast_select_fusion), calls=%async_computation | async-start | bytes 294912 | tf_op jit(solution)/shard_map/all_to_all | solution.py:127
  161.7 72.8 %all-gather.2.cloned.1.call-start = ((), (), s32[]{:S(2)}) async-start(), calls=%async_computation.3 | async-start | bytes 8650752 | tf_op jit(solution)/shard_map/all_gather | solution.py:135
  175.8 197.2 %reduce-scatter.2.cloned.1.call-start = ((), (), s32[]{:S(2)}) async-start(), calls=%async_computation.4 | async-start | bytes 8650752 | tf_op jit(solution)/shard_map/reduce_scatter | solution.py:166
  239.6 10.4 %copy-start.16 = (bf16[4096,128]{1,0:T(8,128)(2,1)S(1)}, bf16[4096,128]{1,0:T(8,128)(2,1)}, u32[]{:S(2)}) copy-start(bf16[4096,128]{1,0:T(8,128)(2,1)} %param.36) | copy-start | bytes 3145732
  250.1 5.9 %copy-start.2 = (bf16[1024,4096]{1,0:T(8,128)(2,1)S(1)}, bf16[1024,4096]{1,0:T(8,128)(2,1)}, u32[]{:S(2)}) copy-start(bf16[1024,4096]{1,0:T(8,128)(2,1)} %multiply_convert_fusion) | copy-start | bytes 25165828
  250.1 6.0 %copy-start.5 = (bf16[4096,128]{1,0:T(8,128)(2,1)S(1)}, bf16[4096,128]{1,0:T(8,128)(2,1)}, u32[]{:S(2)}) copy-start(bf16[4096,128]{1,0:T(8,128)(2,1)} %param.35) | copy-start | bytes 3145732
  256.1 2.9 copy-start.6
  263.7 3.4 copy-start.7
  272.7 102.2 %copy-start.1 = (bf16[5632,128]{1,0:T(8,128)(2,1)S(1)}, bf16[5632,128]{1,0:T(8,128)(2,1)}, u32[]{:S(2)}) copy-start(bf16[5632,128]{1,0:T(8,128)(2,1)} %param.28) | copy-start | bytes 4325380
Sparse Core Ops, SparseCore 0:
  18.3 119.7 all-reduce.4
  175.9 58.5 all-gather.1
  272.9 100.1 reduce-scatter.1
where the time goes:
time: 382 us; the launch traced here: 381 us
  waiting for transfers between devices  261 us (68%)
  other arithmetic  52.5 us (14%)
  matrix products  28.2 us (7%)
  local copies, waits for them, and re-layouts  19 us (5%)
  between operations  13.7 us (4%)
  starting transfers between devices  7.13 us (2%)
    psum x1, waiting for transfers between devices, body(): lax.psum(jnp.dot(hidden, vis_down, preferred_element_type=jnp.float32).as...  107 us
    reduce_scatter x1, waiting for transfers between devices, body(): lax.psum_scatter(jnp.dot(attn_out, out_weight, preferred_element_type=jnp...  88.8 us
    all_gather x1, waiting for transfers between devices, body(): features = lax.all_gather(columns, 'blk', axis=1, tiled=True)  55.5 us
    convert_element_type x1, other arithmetic, body(): token_values = features.astype(jnp.float32)  11.5 us
    convert_element_type x1, other arithmetic, body(): normed_tokens = (token_values * lax.rsqrt(jnp.mean(token_values * token_v...  10.4 us
    all_to_all x1, waiting for transfers between devices, body(): lax.all_to_all(outgoing, 'req', split_axis=0, concat_axis=0, tiled=True)  9.63 us
  transfers between devices with their start and end apart: 4, of which 4 were waited for; matrix products, arithmetic and copies ran while one was open for 7% of the time, Pallas kernels for 0%

commit v1 on v0

--- a/solution.py
+++ b/solution.py
@@ -132,7 +132,9 @@
     columns = jnp.where(
         (lookup < missing)[:, None], jnp.take(row_table, lookup, axis=0), text_embed
     )
-    features = lax.all_gather(columns, "blk", axis=1, tiled=True)
+    features = jnp.concatenate(
+        lax.all_to_all(jnp.stack([columns] * lax.axis_size("blk")), "blk", 0, 0), axis=1
+    )
     token_values = features.astype(jnp.float32)
     normed_tokens = (
         token_values

time: 382 us -> 450 us (1.18)
  waiting for transfers between devices: 261 us -> 319 us
  starting transfers between devices: 7.13 us -> 13.7 us
  local copies, waits for them, and re-layouts: 19 us -> 24 us
    all_to_all x0 -> x1, waiting for transfers between devices: none -> 102 us  [body(): lax.all_to_all(jnp.stack([columns] * lax.axis_size('blk')), 'blk', 0, 0)]
    all_gather x1 -> x0, waiting for transfers between devices: 55.5 us -> none  [body(): features = lax.all_gather(columns, 'blk', axis=1, tiled=True)]
    reduce_scatter x1, waiting for transfers between devices: 88.8 us -> 101 us  [body(): lax.psum_scatter(jnp.dot(attn_out, out_weight, preferred_element_type=jnp...]
    all_to_all x0 -> x1, starting transfers between devices: none -> 6.56 us  [body(): lax.all_to_all(jnp.stack([columns] * lax.axis_size('blk')), 'blk', 0, 0)]
    another operation x2 -> x3, local copies, waits for them, and re-layouts: 0.01 us -> 5.12 us  [the longest x1 5.11 us: body(): jnp.stack([columns] * lax.axis_size('blk'))]
  transfers between devices with their start and end apart: 4 -> 4, of which waited for: 4 -> 4; matrix products, arithmetic and copies ran while one was open for 7% -> 6% of each run, Pallas kernels for 0% -> 0%
where the time goes in v1:
time: 450 us
  waiting for transfers between devices  319 us (71%)
  other arithmetic  50.6 us (11%)
  matrix products  28.2 us (6%)
  local copies, waits for them, and re-layouts  24 us (5%)
  between operations  14 us (3%)
  starting transfers between devices  13.7 us (3%)
    psum x1, waiting for transfers between devices, body(): lax.psum(jnp.dot(hidden, vis_down, preferred_element_type=jnp.float32).as...  107 us
    all_to_all x1, waiting for transfers between devices, body(): lax.all_to_all(jnp.stack([columns] * lax.axis_size('blk')), 'blk', 0, 0)  102 us
    reduce_scatter x1, waiting for transfers between devices, body(): lax.psum_scatter(jnp.dot(attn_out, out_weight, preferred_element_type=jnp...  101 us
    convert_element_type x1, other arithmetic, body(): token_values = features.astype(jnp.float32)  11.4 us
    convert_element_type x1, other arithmetic, body(): normed_tokens = (token_values * lax.rsqrt(jnp.mean(token_values * token_v...  9.77 us
    all_to_all x1, waiting for transfers between devices, body(): lax.all_to_all(outgoing, 'req', split_axis=0, concat_axis=0, tiled=True)  9.69 us
  transfers between devices with their start and end apart: 4, of which 4 were waited for; matrix products, arithmetic and copies ran while one was open for 6% of the time, Pallas kernels for 0%

profile of v1, /device:TPU:2, one launch (start us, length us, event | category | flops | bytes accessed | tf_op | source)
XLA Modules:
  0.0 449.6 jit_solution(8575856272541362861)
XLA Ops:
  9.4 2.3 fusion.10
  11.8 6.3 %convolution_convert_fusion.2 = bf16[768,1408]{1,0:T(8,128)(2,1)} fusion(bf16[192,1408]{1,0:T(8,128)(2,1)S(1)} %copy-done.17, bf16[1408,192]{0,1:T(8,128)(2,1)S(1)} %copy-done.18, bf16[768,1408]{1,0:T(8,128)(2,1)} %param.20, f32[1408]{0:T(1024)S(1)} %convert_element_type.113, f32[1408]{0:T(1024)S(1)} %convert_element_type.112, ...), kind=kOutput, calls=%fused_computation.38 | convolution fusion | flops 847773696 | bytes 5424896 | tf_op jit(solution)/shard_map/dot_general | solution.py:97
  18.4 4.5 %reduce-window.6 = s32[8,8,2,128]{3,1,2,0:T(8,128)S(1)} reduce-window(s32[8,8,2,128]{3,1,2,0:T(8,128)S(1)} %convert_bitcast_fusion.1, s32[]{:T(128)} %constant.42.clone.1), window={size=1x1x1x128 pad=0_0x0_0x0_0x127_0}, to_apply=%region_0.0 | reduce-window | flops 2080768 | bytes 131076 | tf_op jit(solution)/shard_map/reduce-window
  24.8 6.2 %scatter_custom_fusion = s32[1024]{0:T(1024)S(1)} fusion(s32[1536]{0:T(1024)S(1)} %get-tuple-element.80, s32[1536]{0:T(1024)S(1)} %reshape.304, s32[]{:T(128)} %constant.68.clone.1), kind=kCustom, calls=%fused_computation.154 | custom fusion | bytes 4100 | tf_op jit(solution)/shard_map/scatter | solution.py:131
  31.0 107.0 %all-reduce.5.cloned.1.call-done = bf16[768,1408]{1,0:T(8,128)(2,1)} async-done(((bf16[768,1408]{1,0:T(8,128)(2,1)}), bf16[768,1408]{1,0:T(8,128)(2,1)}) %all-reduce.5.cloned.1.call-update) | async-done | bytes 2162704 | tf_op jit(solution)/shard_map/psum | solution.py:96
  138.0 3.2 fusion.17
  142.7 2.4 multiply_convert_fusion.1
  145.1 4.4 reshape.278
  149.6 2.4 fusion.23
  154.7 7.0 %all-to-all-start = ((bf16[8,66,128]{2,1,0:T(8,128)(2,1)}), bf16[8,66,128]{2,1,0:T(8,128)(2,1)S(1)}, u32[]{:S(2)}, u32[]{:S(2)}) async-start(bf16[8,66,128]{2,1,0:T(8,128)(2,1)} %broadcast_select_fusion), calls=%async_computation | async-start | bytes 294912 | tf_op jit(solution)/shard_map/all_to_all | solution.py:127
  161.7 9.7 %all-to-all-done = bf16[8,66,128]{2,1,0:T(8,128)(2,1)S(1)} async-done(((bf16[8,66,128]{2,1,0:T(8,128)(2,1)}), bf16[8,66,128]{2,1,0:T(8,128)(2,1)S(1)}, u32[]{:S(2)}, u32[]{:S(2)}) %all-to-all-start) | async-done | bytes 135200 | tf_op jit(solution)/shard_map/all_to_all | solution.py:127
  171.5 3.2 gather_fusion.1
  175.1 5.1 %stack.2 = bf16[32,1024,128]{2,1,0:T(8,128)(2,1)} broadcast(bf16[1024,128]{1,0:T(8,128)(2,1)S(1)} %select_select_fusion), dimensions={1,2} | broadcast | bytes 8650752 | tf_op jit(solution)/shard_map/stack | solution.py:136
  180.2 6.6 %all-to-all-start.1 = ((bf16[32,1024,128]{2,1,0:T(8,128)(2,1)}), bf16[32,1024,128]{2,1,0:T(8,128)(2,1)}, u32[]{:S(2)}, u32[]{:S(2)}) async-start(bf16[32,1024,128]{2,1,0:T(8,128)(2,1)} %stack.2), calls=%async_computation.1 | async-start | bytes 16777216 | tf_op jit(solution)/shard_map/all_to_all | solution.py:136
  189.7 101.7 %all-to-all-done.1 = bf16[32,1024,128]{2,1,0:T(8,128)(2,1)} async-done(((bf16[32,1024,128]{2,1,0:T(8,128)(2,1)}), bf16[32,1024,128]{2,1,0:T(8,128)(2,1)}, u32[]{:S(2)}, u32[]{:S(2)}) %all-to-all-start.1) | async-done | bytes 8388640 | tf_op jit(solution)/shard_map/all_to_all | solution.py:136
  291.4 5.1 %fusion.7 = f32[1024]{0:T(1024)S(1)} fusion(bf16[32,1024,128]{2,1,0:T(8,128)(2,1)} %all-to-all-done.1), kind=kLoop, calls=%fused_computation.17 | loop fusion | flops 12581888 | bytes 8392704 | tf_op jit(solution)/shard_map/reduce_sum | solution.py:141
  296.5 9.8 %multiply_convert_fusion = bf16[1024,4096]{1,0:T(8,128)(2,1)} fusion(f32[4096]{0:T(1024)S(1)} %convert_element_type.128, f32[1024]{0:T(1024)S(1)} %add_rsqrt_fusion, bf16[32,1024,128]{2,1,0:T(8,128)(2,1)} %all-to-all-done.1), kind=kLoop, calls=%fused_computation.19 | loop fusion | flops 16777216 | bytes 16797696 | tf_op jit(solution)/shard_map/convert_element_type | solution.py:143
  306.3 5.9 %convolution_convert_fusion.3 = bf16[1024,128]{1,0:T(8,128)(2,1)S(1)} fusion(bf16[1024,4096]{1,0:T(8,128)(2,1)} %multiply_convert_fusion, bf16[4096,128]{1,0:T(8,128)(2,1)S(1)} %copy-done.16), kind=kOutput, calls=%fused_computation.44 | convolution fusion | flops 1073872896 | bytes 9699328 | tf_op jit(solution)/shard_map/dot_general | solution.py:151
  312.3 2.9 convolution_bitcast_fusion
  315.2 2.9 convolution_bitcast_fusion.1
  319.7 3.6 while.10
  323.4 5.5 %convolution_convert_fusion.1 = bf16[1024,4096]{1,0:T(8,128)(2,1)} fusion(bf16[1024,128]{1,0:T(8,128)(2,1)S(1)} %bitcast.79, bf16[128,4096]{1,0:T(8,128)(2,1)S(1)} %copy-done.7), kind=kOutput, calls=%fused_computation.20 | convolution fusion | flops 1077936128 | bytes 9699328 | tf_op jit(solution)/shard_map/dot_general | solution.py:169
  329.0 11.4 %copy_bitcast_fusion = f32[1024,4096]{1,0:T(8,128)} fusion(bf16[32,1024,128]{2,1,0:T(8,128)(2,1)} %all-to-all-done.1), kind=kLoop, calls=%fused_computation.18 | loop fusion | flops 4194304 | bytes 25165824 | tf_op jit(solution)/shard_map/convert_element_type | solution.py:138
  340.4 100.5 %reduce-scatter.2.cloned.1.call-done = bf16[32,4096]{1,0:T(8,128)(2,1)} async-done(((bf16[1024,4096]{1,0:T(8,128)(2,1)}), bf16[32,4096]{1,0:T(8,128)(2,1)}) %reduce-scatter.2.cloned.1.call-update) | async-done | bytes 262160 | tf_op jit(solution)/shard_map/reduce_scatter | solution.py:168
  (109 shorter events, 19.4 us)
Async XLA Ops:
  6.5 143.0 %copy-start = (bf16[5632,128]{1,0:T(8,128)(2,1)S(1)}, bf16[5632,128]{1,0:T(8,128)(2,1)}, u32[]{:S(2)}) copy-start(bf16[5632,128]{1,0:T(8,128)(2,1)} %param.28) | copy-start | bytes 4325380
  6.5 5.2 %copy-start.12 = (bf16[1408]{0:T(1024)(128)(2,1)S(1)}, bf16[1408]{0:T(1024)(128)(2,1)}, u32[]{:S(2)}) copy-start(bf16[1408]{0:T(1024)(128)(2,1)} %param.21) | copy-start | bytes 8452
  6.5 5.2 %copy-start.13 = (bf16[1408]{0:T(1024)(128)(2,1)S(1)}, bf16[1408]{0:T(1024)(128)(2,1)}, u32[]{:S(2)}) copy-start(bf16[1408]{0:T(1024)(128)(2,1)} %param.22) | copy-start | bytes 8452
  6.5 5.2 %copy-start.17 = (bf16[192,1408]{1,0:T(8,128)(2,1)S(1)}, bf16[192,1408]{1,0:T(8,128)(2,1)}, u32[]{:S(2)}) copy-start(bf16[192,1408]{1,0:T(8,128)(2,1)} %param.25) | copy-start | bytes 1622020
  6.5 5.2 %copy-start.18 = (bf16[1408,192]{0,1:T(8,128)(2,1)S(1)}, bf16[1408,192]{0,1:T(8,128)(2,1)}, u32[]{:S(2)}) copy-start(bf16[1408,192]{0,1:T(8,128)(2,1)} %param.23) | copy-start | bytes 1622020
  6.5 131.5 %all-reduce.5.cloned.1.call-start = ((), (), s32[]{:S(2)}) async-start(), calls=%async_computation.3 | async-start | bytes 4325376 | tf_op jit(solution)/shard_map/psum | solution.py:96
  11.8 6.4 %copy-start.19 = (bf16[128]{0:T(256)(128)(2,1)S(1)}, bf16[128]{0:T(256)(128)(2,1)}, u32[]{:S(2)}) copy-start(bf16[128]{0:T(256)(128)(2,1)} %param.29) | copy-start | bytes 772
  11.8 6.4 %copy-start.14 = (bf16[1408]{0:T(1024)(128)(2,1)S(1)}, bf16[1408]{0:T(1024)(128)(2,1)}, u32[]{:S(2)}) copy-start(bf16[1408]{0:T(1024)(128)(2,1)} %param.26) | copy-start | bytes 8452
  11.8 6.4 %copy-start.15 = (bf16[1408]{0:T(1024)(128)(2,1)S(1)}, bf16[1408]{0:T(1024)(128)(2,1)}, u32[]{:S(2)}) copy-start(bf16[1408]{0:T(1024)(128)(2,1)} %param.27) | copy-start | bytes 8452
  11.8 6.4 %copy-start.10 = (s32[1536]{0:T(1024)S(1)}, s32[1536]{0:T(1024)}, u32[]{:S(2)}) copy-start(s32[1536]{0:T(1024)} %param.30) | copy-start | bytes 18436
  138.0 3.2 copy-start.3
  138.0 3.6 copy-start.4
  149.5 25.2 %copy-start.8 = (bf16[1024,128]{1,0:T(8,128)(2,1)S(1)}, bf16[1024,128]{1,0:T(8,128)(2,1)}, u32[]{:S(2)}) copy-start(bf16[1024,128]{1,0:T(8,128)(2,1)} %param.31) | copy-start | bytes 786436
  154.7 16.7 %all-to-all-start = ((bf16[8,66,128]{2,1,0:T(8,128)(2,1)}), bf16[8,66,128]{2,1,0:T(8,128)(2,1)S(1)}, u32[]{:S(2)}, u32[]{:S(2)}) async-start(bf16[8,66,128]{2,1,0:T(8,128)(2,1)} %broadcast_select_fusion), calls=%async_computation | async-start | bytes 294912 | tf_op jit(solution)/shard_map/all_to_all | solution.py:127
  180.2 7.1 %copy-start.9 = (s32[1,1024]{1,0:T(1,128)S(1)}, s32[1,1024]{1,0:T(1,128)}, u32[]{:S(2)}) copy-start(s32[1,1024]{1,0:T(1,128)} %param.32) | copy-start | bytes 12292
  180.2 8.3 %copy-start.11 = (bf16[4096]{0:T(1024)(128)(2,1)S(1)}, bf16[4096]{0:T(1024)(128)(2,1)}, u32[]{:S(2)}) copy-start(bf16[4096]{0:T(1024)(128)(2,1)} %param.33) | copy-start | bytes 24580
  180.2 111.2 %all-to-all-start.1 = ((bf16[32,1024,128]{2,1,0:T(8,128)(2,1)}), bf16[32,1024,128]{2,1,0:T(8,128)(2,1)}, u32[]{:S(2)}, u32[]{:S(2)}) async-start(bf16[32,1024,128]{2,1,0:T(8,128)(2,1)} %stack.2), calls=%async_computation.1 | async-start | bytes 16777216 | tf_op jit(solution)/shard_map/all_to_all | solution.py:136
  186.8 254.1 %reduce-scatter.2.cloned.1.call-start = ((), (), s32[]{:S(2)}) async-start(), calls=%async_computation.4 | async-start | bytes 8650752 | tf_op jit(solution)/shard_map/reduce_scatter | solution.py:168
  296.5 9.8 %copy-start.16 = (bf16[4096,128]{1,0:T(8,128)(2,1)S(1)}, bf16[4096,128]{1,0:T(8,128)(2,1)}, u32[]{:S(2)}) copy-start(bf16[4096,128]{1,0:T(8,128)(2,1)} %param.36) | copy-start | bytes 3145732
  306.3 5.9 %copy-start.2 = (bf16[1024,4096]{1,0:T(8,128)(2,1)S(1)}, bf16[1024,4096]{1,0:T(8,128)(2,1)}, u32[]{:S(2)}) copy-start(bf16[1024,4096]{1,0:T(8,128)(2,1)} %multiply_convert_fusion) | copy-start | bytes 25165828
  306.3 6.0 %copy-start.5 = (bf16[4096,128]{1,0:T(8,128)(2,1)S(1)}, bf16[4096,128]{1,0:T(8,128)(2,1)}, u32[]{:S(2)}) copy-start(bf16[4096,128]{1,0:T(8,128)(2,1)} %param.35) | copy-start | bytes 3145732
  312.3 2.9 copy-start.6
  319.7 3.7 copy-start.7
  328.9 113.8 %copy-start.1 = (bf16[5632,128]{1,0:T(8,128)(2,1)S(1)}, bf16[5632,128]{1,0:T(8,128)(2,1)}, u32[]{:S(2)}) copy-start(bf16[5632,128]{1,0:T(8,128)(2,1)} %param.28) | copy-start | bytes 4325380
Sparse Core Ops, SparseCore 0:
  18.3 119.7 all-reduce.4
  329.1 111.7 reduce-scatter.1
